TPU v7x, 256 devices: a whole 4x4x8 slice. The times are simulated.
256 devices in a mesh: seq: 32 (over x, y, core), exp: 8 (over z).
Axes of the slice: x: 4, y: 4, z: 8, core: 2. Of those that a mesh axis runs over, the one named last changes fastest.
Arguments:
- query_rows: bfloat16 [2048, 8192], P('seq', 'exp'), may hold values from -6 to 6
- key_rows: bfloat16 [2048, 8192], P('seq', 'exp'), may hold values from -6 to 6
- value_rows: bfloat16 [2048, 8192], P('seq', 'exp'), may hold values from -120 to 120
- log_decay: float32 [2048, 64], P('seq', 'exp'), may hold values from -1.4625 to 0, as said below
- out_weight: bfloat16 [8192, 6144], P('exp', 'seq'), may hold values from -0.0625 to 0.0625
- residual: bfloat16 [2048, 6144], P('exp', 'seq'), may hold values from -18 to 18
- routes: int32 [2048, 2], P('exp'), may hold values from 0 to 7, all different within a row; in each aligned block of 256 rows (0 to 255, 256 to 511, ...) at most 128 rows name the same one
- gate_weight: bfloat16 [8, 9216, 6144], P('exp', 'seq'), may hold values from -0.078125 to 0.078125
- up_weight: bfloat16 [8, 9216, 6144], P('exp', 'seq'), may hold values from -0.078125 to 0.078125
Outputs:
- residual_out: bfloat16 [2048, 6144], P('exp', 'seq')
- expert_hidden: bfloat16 [8, 9216, 1024], P('exp', 'seq')
Inputs may be any that keep to these rules, and one draw needn't show every extreme that they name: `routes`: each token names 2 different experts; within one source group of 256 tokens no expert is named more than 128 times. `log_decay`: every entry is negative.
All inputs are finite; a program needn't handle non-finite values.
Results may differ from a plain program's by a relative error of at most 0.0065.
Values may be sent and summed in bfloat16 or wider, within the bound.
No kernel may reach another device: no remote copies, remote signals or barrier semaphores. Data moves between devices by JAX's collectives and lax.ppermute only.
A program may use at most 128 MiB of HBM per device.

v0:
```python
import jax
import jax.numpy as jnp
from jax import lax
from jax.sharding import Mesh
from jax.sharding import PartitionSpec as P

D = 6144
HEAD_DIM = 128
SEQ = ("seq_0", "seq_1", "seq_2")
precise = lax.Precision.HIGHEST
contract_last = (((1,), (1,)), ((), ()))


def nothing_yet(shard, identity):
    return jax.tree.map(
        lambda a, e: jnp.broadcast_to(jnp.asarray(e, a.dtype), a.shape), shard, identity
    )


def carried_in(shard, axes, combine, identity):
    before = start = nothing_yet(shard, identity)
    so_far = shard
    for axis in reversed(axes):
        peers, place = (lax.axis_size(axis), lax.axis_index(axis))
        pieces = jax.tree.map(lambda part: lax.all_gather(part, axis), so_far)
        inside, so_far = (start, start)
        for k in range(peers):
            passed = k < place
            so_far = combine(so_far, jax.tree.map(lambda part: part[k], pieces))
            inside = jax.tree.map(lambda new, old: jnp.where(passed, new, old), so_far, inside)
        before = combine(inside, before)
    return before


def link_states(earlier, later):
    return (earlier[0] * later[0], later[0][:, None, None] * earlier[1] + later[1])


def swap_cores(tree):
    return jax.tree.map(lambda part: lax.ppermute(part, "seq_2", [(0, 1), (1, 0)]), tree)


def prefix_over(own, axis):
    peers, place = (lax.axis_size(axis), lax.axis_index(axis))
    shifted = [own] + [
        jax.tree.map(
            lambda part: lax.ppermute(part, axis, [(i, (i + d) % peers) for i in range(peers)]), own
        )
        for d in range(1, peers)
    ]
    start = nothing_yet(own, (1.0, 0.0))
    before, total = (start, start)
    for k in range(peers):
        lag = (place - k) % peers
        piece = jax.tree.map(
            lambda *opts: jnp.select([lag == d for d in range(peers)], opts), *shifted
        )
        total = link_states(total, piece)
        passed = k < place
        before = jax.tree.map(lambda new, old: jnp.where(passed, new, old), total, before)
    return (before, total)


def entering_state(decay, state):
    core = lax.axis_index("seq_2")
    other = swap_cores((decay, state))
    first = jax.tree.map(
        lambda mine, theirs: jnp.where(core == 0, mine, theirs), (decay, state), other
    )
    second = jax.tree.map(
        lambda mine, theirs: jnp.where(core == 0, theirs, mine), (decay, state), other
    )
    chip = link_states(first, second)
    half = decay.shape[0] // 2
    mine = jax.tree.map(lambda part: lax.dynamic_slice_in_dim(part, core * half, half, 0), chip)
    along_y, row = prefix_over(mine, "seq_1")
    along_x, _ = prefix_over(row, "seq_0")
    chip_before = link_states(along_x, along_y)
    theirs = swap_cores(chip_before)
    whole = jax.tree.map(
        lambda a, b: jnp.where(core == 0, jnp.concatenate([a, b], 0), jnp.concatenate([b, a], 0)),
        chip_before,
        theirs,
    )
    return jnp.where(core == 0, whole[1], first[0][:, None, None] * whole[1] + first[1])


def finish_rows(gate_sum, up_sum, squares):
    inv_rms = lax.rsqrt(squares / D + 1e-06)[None, :]
    return (jax.nn.silu(gate_sum * inv_rms) * (up_sum * inv_rms)).astype(jnp.bfloat16)


def body(
    query_rows,
    key_rows,
    value_rows,
    log_decay,
    out_weight,
    residual,
    routes,
    gate_weight,
    up_weight,
):
    positions, head_cols = query_rows.shape
    heads_here = head_cols // HEAD_DIM
    queries = query_rows.astype(jnp.float32).reshape(positions, heads_here, HEAD_DIM)
    keys_here = key_rows.astype(jnp.float32).reshape(positions, heads_here, HEAD_DIM)
    values_here = value_rows.astype(jnp.float32).reshape(positions, heads_here, HEAD_DIM)
    cumulative = jnp.cumsum(log_decay, axis=0)
    closing = cumulative[-1]
    key_scaled = keys_here * jnp.exp(closing[None, :] - cumulative)[:, :, None]
    local_state = jnp.einsum("shd,she->hde", key_scaled, values_here, precision=precise)
    entering = entering_state(jnp.exp(closing), local_state)
    later = lax.broadcasted_iota(jnp.int32, (positions, positions), 0)
    earlier = lax.broadcasted_iota(jnp.int32, (positions, positions), 1)
    causal = (later >= earlier)[None]
    carried = jnp.einsum(
        "thd,hde->the", queries * jnp.exp(cumulative)[:, :, None], entering, precision=precise
    )
    scores = jnp.einsum("thd,shd->hts", queries, keys_here, precision=precise)
    spread = cumulative.T[:, :, None] - cumulative.T[:, None, :]
    weights = jnp.where(causal, jnp.exp(jnp.where(causal, spread, 0.0)), 0.0)
    within = jnp.einsum("hts,she->the", scores * weights, values_here, precision=precise)
    head_raw = carried + within
    normed = head_raw * lax.rsqrt(jnp.mean(head_raw * head_raw, axis=-1, keepdims=True) + 1e-06)
    normed = normed.astype(jnp.bfloat16).reshape(positions, head_cols)
    gathered = lax.all_gather(normed, SEQ, axis=0, tiled=True)
    row_block = gathered
    attended = lax.psum_scatter(
        jnp.dot(row_block, out_weight, preferred_element_type=jnp.float32),
        "exp",
        scatter_dimension=0,
        tiled=True,
    )
    residual_out = (residual.astype(jnp.float32) + attended).astype(jnp.bfloat16)
    group_rows = routes.shape[0]
    choices_each = routes.shape[1]
    experts = lax.axis_size("exp")
    capacity = 4 * group_rows // experts
    route_flat = routes.reshape(-1)
    expert_ids = lax.broadcasted_iota(jnp.int32, (1, experts), 1)
    onehot = (route_flat[:, None] == expert_ids).astype(jnp.int32)
    slot_index = jnp.sum(jnp.cumsum(onehot, axis=0) * onehot, axis=1) - 1
    target = route_flat * capacity + slot_index
    w_gate = gate_weight[0]
    w_up = up_weight[0]
    hidden_rows = w_gate.shape[0]
    columns = residual_out.shape[1]
    buffer = jnp.zeros((experts * capacity, columns), jnp.bfloat16)
    buffer = buffer.at[target].set(jnp.repeat(residual_out, choices_each, axis=0))
    received = lax.all_to_all(
        buffer.reshape(experts, capacity, columns), "exp", split_axis=0, concat_axis=0, tiled=True
    )
    sources, entries, gathered_columns = received.shape
    slices = received.reshape(sources * entries, gathered_columns)
    row_block = lax.all_gather(slices, SEQ, axis=1, tiled=True)
    squares = jnp.einsum("rd,rd->r", row_block, row_block, preferred_element_type=jnp.float32)
    gate_sum = lax.dot_general(w_gate, row_block, contract_last, preferred_element_type=jnp.float32)
    up_sum = lax.dot_general(w_up, row_block, contract_last, preferred_element_type=jnp.float32)
    expert_hidden = finish_rows(gate_sum, up_sum, squares).reshape(hidden_rows, sources, entries)
    return (residual_out, expert_hidden.reshape(1, hidden_rows, experts * capacity))


def solution(mesh):
    torus = Mesh(
        mesh.devices.reshape(4, 4, 2, mesh.shape["exp"]), ("seq_0", "seq_1", "seq_2", "exp")
    )
    in_specs = (
        P(SEQ, "exp"),
        P(SEQ, "exp"),
        P(SEQ, "exp"),
        P(SEQ, "exp"),
        P("exp", SEQ),
        P("exp", SEQ),
        P("exp", None),
        P("exp", SEQ, None),
        P("exp", SEQ, None),
    )
    out_specs = (P("exp", SEQ), P("exp", SEQ, None))
    return jax.shard_map(body, mesh=torus, in_specs=in_specs, out_specs=out_specs, check_vma=False)
```

profile of v0, /device:TPU:1, one launch (start us, length us, event | category | flops | bytes accessed | tf_op | source)
XLA Modules:
  0.0 311.5 jit_solution(16042389560862939219)
XLA Ops:
  10.9 3.2 %collective-permute-start = (f32[8]{0:T(128)S(1)}, f32[8]{0:T(128)S(1)}, u32[]{:S(2)}, u32[]{:S(2)}) collective-permute-start(f32[8]{0:T(128)S(1)} %fusion.59), channel_id=1, source_target_pairs={{0,8},{8,0},{1,9},{9,1},{2,10},{10,2},{3,11},{11,3},{4,12},{12,4},... | collective-permute-start | bytes 104 | tf_op jit(solution)/shard_map/ppermute | solution.py:40
  17.0 2.4 fusion.36
  49.0 2.3 collective-permute-start.3
  55.4 2.5 collective-permute-start.6
  58.5 1.9 collective-permute-done.10
  62.0 7.3 %collective-permute-done.8 = f32[4,128,128]{2,1,0:T(8,128)S(1)} collective-permute-done((f32[4,128,128]{2,1,0:T(8,128)S(1)}, f32[4,128,128]{2,1,0:T(8,128)S(1)}, u32[]{:S(2)}, u32[]{:S(2)}) %collective-permute-start.8) | collective-permute-done | bytes 262176 | tf_op jit(solution)/shard_map/ppermute | solution.py:47
  69.6 2.8 collective-permute-start.12
  72.8 2.4 collective-permute-start.13
  75.2 3.5 %collective-permute-done.12 = f32[4,128,128]{2,1,0:T(8,128)S(1)} collective-permute-done((f32[4,128,128]{2,1,0:T(8,128)S(1)}, f32[4,128,128]{2,1,0:T(8,128)S(1)}, u32[]{:S(2)}, u32[]{:S(2)}) %collective-permute-start.12) | collective-permute-done | bytes 262176 | tf_op jit(solution)/shard_map/ppermute | solution.py:47
  78.6 6.4 %collective-permute-done.11 = f32[4,128,128]{2,1,0:T(8,128)S(1)} collective-permute-done((f32[4,128,128]{2,1,0:T(8,128)S(1)}, f32[4,128,128]{2,1,0:T(8,128)S(1)}, u32[]{:S(2)}, u32[]{:S(2)}) %collective-permute-start.11) | collective-permute-done | bytes 262176 | tf_op jit(solution)/shard_map/ppermute | solution.py:47
  90.1 2.2 multiply_reduce_fusion
  93.2 51.6 %all-gather.3.cloned.1.call-done = bf16[2048,1024]{1,0:T(8,128)(2,1)} async-done(((bf16[64,1024]{1,0:T(8,128)(2,1)}), bf16[2048,1024]{1,0:T(8,128)(2,1)}) %all-gather.3.cloned.1.call-update) | async-done | bytes 4194320 | tf_op jit(solution)/shard_map/all_gather | solution.py:127
  144.8 5.0 %fusion.62 = f32[2048,192]{0,1:T(8,128)} fusion(bf16[2048,1024]{1,0:T(8,128)(2,1)} %all-gather.3.cloned.1.call-done, bf16[1024,192]{0,1:T(8,128)(2,1)} %param.13), kind=kOutput, calls=%fused_computation.128 | convolution fusion | flops 805306368 | bytes 6160384 | tf_op jit(solution)/shard_map/dot_general | solution.py:130
  156.3 2.2 reduce-window.6
  162.8 22.7 %reduce-scatter.2.cloned.1.call-done = f32[256,192]{0,1:T(8,128)} async-done(((f32[2048,192]{0,1:T(8,128)}), f32[256,192]{0,1:T(8,128)}) %reduce-scatter.2.cloned.1.call-update) | async-done | bytes 196624 | tf_op jit(solution)/shard_map/reduce_scatter | solution.py:129
  188.7 1.7 broadcast_in_dim.122
  190.5 1.9 reshape.145
  192.3 3.5 %scatter_custom_fusion = bf16[1024,192]{1,0:T(8,128)(2,1)} fusion(s32[512]{0:T(512)S(1)} %bitcast.151, bf16[512,192]{1,0:T(8,128)(2,1)} %reshape.145, bf16[]{:T(256)} %constant.147.clone.1), kind=kCustom, calls=%fused_computation.26 | custom fusion | bytes 393728 | tf_op jit(solution)/shard_map/scatter | solution.py:150
  195.9 2.0 copy.86
  197.9 15.8 %all_to_all.5 = bf16[8,128,192]{1,2,0:T(8,128)(2,1)S(1)} all-to-all(bf16[8,128,192]{1,2,0:T(8,128)(2,1)} %copy.86), channel_id=1, replica_groups=mesh['seq_0'=4,'seq_1'=4,'seq_2'=2,'exp'=8] {'exp'}, dimensions={0} | all-to-all | bytes 786432 | tf_op jit(solution)/shard_map/all_to_all | solution.py:151
  214.5 69.3 %all-gather.5.cloned.1.call-done = bf16[1024,6144]{0,1:T(8,128)(2,1)} async-done(((bf16[1024,192]{0,1:T(8,128)(2,1)}), bf16[1024,6144]{0,1:T(8,128)(2,1)}) %all-gather.5.cloned.1.call-update) | async-done | bytes 12582928 | tf_op jit(solution)/shard_map/all_gather | solution.py:156
  283.8 7.1 %fusion = f32[1024]{0:T(1024)S(1)} fusion(bf16[1024,6144]{0,1:T(8,128)(2,1)} %all-gather.5.cloned.1.call-done), kind=kLoop, calls=%fused_computation.2 | loop fusion | flops 18873344 | bytes 12587008 | tf_op jit(solution)/shard_map/rd,rd->r/dot_general | solution.py:157
  290.9 7.0 %fusion.17 = f32[288,1024]{1,0:T(8,128)S(1)} fusion(bf16[1024,6144]{0,1:T(8,128)(2,1)} %all-gather.5.cloned.1.call-done, bf16[1,288,6144]{2,1,0:T(8,128)(2,1)S(1)} %copy-done, f32[1024]{0:T(1024)S(1)} %add_rsqrt_fusion), kind=kOutput, calls=%fused_computation.11 | convolution fusion | flops 3624173568 | bytes 17305600 | tf_op jit(solution)/shard_map/dot_general | solution.py:158
  300.1 4.9 %fusion.23 = bf16[1,288,1024]{2,1,0:T(8,128)(2,1)} fusion(bf16[1024,6144]{0,1:T(8,128)(2,1)S(1)} %copy-done.1, bf16[1,288,6144]{2,1,0:T(8,128)(2,1)S(1)} %copy-done.5, f32[288,1024]{1,0:T(8,128)S(1)} %fusion.17, f32[1024]{0:T(1024)S(1)} %add_rsqrt_fusion), kind=kOutput, calls=%fused_computation.13 | convolution fusion | flops 3625943040 | bytes 17895424 | tf_op jit(solution)/shard_map/dot_general | solution.py:159
  (98 shorter events, 46.2 us)
Async XLA Ops:
  7.2 283.7 %copy-start = (bf16[1,288,6144]{2,1,0:T(8,128)(2,1)S(1)}, bf16[1,288,6144]{2,1,0:T(8,128)(2,1)}, u32[]{:S(2)}) copy-start(bf16[1,288,6144]{2,1,0:T(8,128)(2,1)} %param.16) | copy-start | bytes 10616836
  7.2 137.6 %all-gather.3.cloned.1.call-start = ((), (), s32[]{:S(2)}) async-start(), calls=%async_computation.2 | async-start | bytes 4325376 | tf_op jit(solution)/shard_map/all_gather | solution.py:127
  10.9 35.7 %collective-permute-start = (f32[8]{0:T(128)S(1)}, f32[8]{0:T(128)S(1)}, u32[]{:S(2)}, u32[]{:S(2)}) collective-permute-start(f32[8]{0:T(128)S(1)} %fusion.59), channel_id=1, source_target_pairs={{0,8},{8,0},{1,9},{9,1},{2,10},{10,2},{3,11},{11,3},{4,12},{12,4},... | collective-permute-start | bytes 104 | tf_op jit(solution)/shard_map/ppermute | solution.py:40
  19.5 31.9 %collective-permute-start.7 = (f32[8,128,128]{2,1,0:T(8,128)}, f32[8,128,128]{2,1,0:T(8,128)}, u32[]{:S(2)}, u32[]{:S(2)}) collective-permute-start(f32[8,128,128]{2,1,0:T(8,128)} %fusion.36), channel_id=1, source_target_pairs={{0,8},{8,0},{1,9},{9,1},{2,10},{10,2},{3,11},{11,3},{4,12},{12,4},... | collective-permute-start | bytes 1572872 | tf_op jit(solution)/shard_map/ppermute | solution.py:40
  46.6 40.5 %copy-start.3 = (bf16[64,1024]{1,0:T(8,128)(2,1)S(1)}, bf16[64,1024]{1,0:T(8,128)(2,1)}, u32[]{:S(2)}) copy-start(bf16[64,1024]{1,0:T(8,128)(2,1)} %param.10) | copy-start | bytes 393220
  46.6 40.5 %copy-start.6 = (bf16[64,1024]{1,0:T(8,128)(2,1)S(1)}, bf16[64,1024]{1,0:T(8,128)(2,1)}, u32[]{:S(2)}) copy-start(bf16[64,1024]{1,0:T(8,128)(2,1)} %param.9) | copy-start | bytes 393220
  47.4 7.4 %collective-permute-start.2 = (f32[4]{0:T(128)S(1)}, f32[4]{0:T(128)S(1)}, u32[]{:S(2)}, u32[]{:S(2)}) collective-permute-start(f32[4]{0:T(128)S(1)} %dynamic_slice.6), channel_id=1, source_target_pairs={{0,32},{16,48},{32,0},{48,16},{1,33},{17,49},{33,1},{49,17},{2,34}... | collective-permute-start | bytes 56 | tf_op jit(solution)/shard_map/ppermute | solution.py:47
  48.6 6.7 %collective-permute-start.1 = (f32[4]{0:T(128)S(1)}, f32[4]{0:T(128)S(1)}, u32[]{:S(2)}, u32[]{:S(2)}) collective-permute-start(f32[4]{0:T(128)S(1)} %dynamic_slice.6), channel_id=1, source_target_pairs={{0,16},{16,32},{32,48},{48,0},{1,17},{17,33},{33,49},{49,1},{2,18}... | collective-permute-start | bytes 56 | tf_op jit(solution)/shard_map/ppermute | solution.py:47
  49.0 6.3 %collective-permute-start.3 = (f32[4]{0:T(128)S(1)}, f32[4]{0:T(128)S(1)}, u32[]{:S(2)}, u32[]{:S(2)}) collective-permute-start(f32[4]{0:T(128)S(1)} %dynamic_slice.6), channel_id=1, source_target_pairs={{0,48},{16,0},{32,16},{48,32},{1,49},{17,1},{33,17},{49,33},{2,50}... | collective-permute-start | bytes 56 | tf_op jit(solution)/shard_map/ppermute | solution.py:47
  52.5 16.9 %copy-start.2 = (f32[8,128,128]{2,1,0:T(8,128)}, f32[8,128,128]{2,1,0:T(8,128)S(1)}, u32[]{:S(2)}) copy-start(f32[8,128,128]{2,1,0:T(8,128)S(1)} %broadcast_select_fusion) | copy-start | bytes 1572868
  53.8 6.5 %collective-permute-start.10 = (f32[4,128,128]{2,1,0:T(8,128)S(1)}, f32[4,128,128]{2,1,0:T(8,128)S(1)}, u32[]{:S(2)}, u32[]{:S(2)}) collective-permute-start(f32[4,128,128]{2,1,0:T(8,128)S(1)} %fusion.30), channel_id=1, source_target_pairs={{0,48},{16,0},{32,16},{48,32},{1,49},{17,1},{33,17},{49,33},{2,50}... | collective-permute-start | bytes 786440 | tf_op jit(solution)/shard_map/ppermute | solution.py:47
  53.9 8.1 %collective-permute-start.9 = (f32[4,128,128]{2,1,0:T(8,128)S(1)}, f32[4,128,128]{2,1,0:T(8,128)S(1)}, u32[]{:S(2)}, u32[]{:S(2)}) collective-permute-start(f32[4,128,128]{2,1,0:T(8,128)S(1)} %fusion.30), channel_id=1, source_target_pairs={{0,32},{16,48},{32,0},{48,16},{1,33},{17,49},{33,1},{49,17},{2,34}... | collective-permute-start | bytes 786440 | tf_op jit(solution)/shard_map/ppermute | solution.py:47
  54.9 14.5 %collective-permute-start.8 = (f32[4,128,128]{2,1,0:T(8,128)S(1)}, f32[4,128,128]{2,1,0:T(8,128)S(1)}, u32[]{:S(2)}, u32[]{:S(2)}) collective-permute-start(f32[4,128,128]{2,1,0:T(8,128)S(1)} %fusion.30), channel_id=1, source_target_pairs={{0,16},{16,32},{32,48},{48,0},{1,17},{17,33},{33,49},{49,1},{2,18}... | collective-permute-start | bytes 786440 | tf_op jit(solution)/shard_map/ppermute | solution.py:47
  55.4 17.3 %collective-permute-start.6 = (f32[4]{0:T(128)S(1)}, f32[4]{0:T(128)S(1)}, u32[]{:S(2)}, u32[]{:S(2)}) collective-permute-start(f32[4]{0:T(128)S(1)} %get-tuple-element.19), channel_id=1, source_target_pairs={{0,192},{64,0},{128,64},{192,128},{1,193},{65,1},{129,65},{193,129... | collective-permute-start | bytes 56 | tf_op jit(solution)/shard_map/ppermute | solution.py:47
  57.9 17.2 %collective-permute-start.5 = (f32[4]{0:T(128)S(1)}, f32[4]{0:T(128)S(1)}, u32[]{:S(2)}, u32[]{:S(2)}) collective-permute-start(f32[4]{0:T(128)S(1)} %get-tuple-element.19), channel_id=1, source_target_pairs={{0,128},{64,192},{128,0},{192,64},{1,129},{65,193},{129,1},{193,65... | collective-permute-start | bytes 56 | tf_op jit(solution)/shard_map/ppermute | solution.py:47
  60.3 14.8 %collective-permute-start.4 = (f32[4]{0:T(128)S(1)}, f32[4]{0:T(128)S(1)}, u32[]{:S(2)}, u32[]{:S(2)}) collective-permute-start(f32[4]{0:T(128)S(1)} %get-tuple-element.19), channel_id=1, source_target_pairs={{0,64},{64,128},{128,192},{192,0},{1,65},{65,129},{129,193},{193,1... | collective-permute-start | bytes 56 | tf_op jit(solution)/shard_map/ppermute | solution.py:47
  69.6 9.0 %collective-permute-start.12 = (f32[4,128,128]{2,1,0:T(8,128)S(1)}, f32[4,128,128]{2,1,0:T(8,128)S(1)}, u32[]{:S(2)}, u32[]{:S(2)}) collective-permute-start(f32[4,128,128]{2,1,0:T(8,128)S(1)} %select_add_fusion.1), channel_id=1, source_target_pairs={{0,128},{64,192},{128,0},{192,64},{1,129},{65,193},{129,1},{193,65... | collective-permute-start | bytes 786440 | tf_op jit(solution)/shard_map/ppermute | solution.py:47
  72.4 12.6 %collective-permute-start.11 = (f32[4,128,128]{2,1,0:T(8,128)S(1)}, f32[4,128,128]{2,1,0:T(8,128)S(1)}, u32[]{:S(2)}, u32[]{:S(2)}) collective-permute-start(f32[4,128,128]{2,1,0:T(8,128)S(1)} %select_add_fusion.1), channel_id=1, source_target_pairs={{0,64},{64,128},{128,192},{192,0},{1,65},{65,129},{129,193},{193,1... | collective-permute-start | bytes 786440 | tf_op jit(solution)/shard_map/ppermute | solution.py:47
  72.8 12.3 %collective-permute-start.13 = (f32[4,128,128]{2,1,0:T(8,128)S(1)}, f32[4,128,128]{2,1,0:T(8,128)S(1)}, u32[]{:S(2)}, u32[]{:S(2)}) collective-permute-start(f32[4,128,128]{2,1,0:T(8,128)S(1)} %select_add_fusion.1), channel_id=1, source_target_pairs={{0,192},{64,0},{128,64},{192,128},{1,193},{65,1},{129,65},{193,129... | collective-permute-start | bytes 786440 | tf_op jit(solution)/shard_map/ppermute | solution.py:47
  86.5 3.6 %collective-permute-start.14 = (f32[4,128,128]{2,1,0:T(8,128)}, f32[4,128,128]{2,1,0:T(8,128)}, u32[]{:S(2)}, u32[]{:S(2)}) collective-permute-start(f32[4,128,128]{2,1,0:T(8,128)} %select_add_fusion), channel_id=1, source_target_pairs={{0,8},{8,0},{1,9},{9,1},{2,10},{10,2},{3,11},{11,3},{4,12},{12,4},... | collective-permute-start | bytes 786440 | tf_op jit(solution)/shard_map/ppermute | solution.py:40
  93.1 56.7 %copy-start.4 = (s32[256,2]{0,1:T(2,128)S(1)}, s32[256,2]{0,1:T(2,128)}, u32[]{:S(2)}) copy-start(s32[256,2]{0,1:T(2,128)} %param.15) | copy-start | bytes 6148
  93.1 92.3 %reduce-scatter.2.cloned.1.call-start = ((), (), s32[]{:S(2)}) async-start(), calls=%async_computation.3 | async-start | bytes 1769472 | tf_op jit(solution)/shard_map/reduce_scatter | solution.py:129
  149.8 134.0 %all-gather.5.cloned.1.call-start = ((), (), s32[]{:S(2)}) async-start(), calls=%async_computation.4 | async-start | bytes 12976128 | tf_op jit(solution)/shard_map/all_gather | solution.py:156
  290.9 9.2 %copy-start.5 = (bf16[1,288,6144]{2,1,0:T(8,128)(2,1)S(1)}, bf16[1,288,6144]{2,1,0:T(8,128)(2,1)}, u32[]{:S(2)}) copy-start(bf16[1,288,6144]{2,1,0:T(8,128)(2,1)} %param.17) | copy-start | bytes 10616836
  (1 other events, 8.2 us)
Sparse Core Ops, SparseCore 0:
  93.2 51.5 all-gather.2
  149.9 35.4 reduce-scatter.1
  214.6 69.1 all-gather.4
where the time goes:
time: 313 us; the launch traced here: 311 us
  waiting for transfers between devices  163 us (52%)
  between operations  33.7 us (11%)
  other arithmetic  28.5 us (9%)
  local copies, waits for them, and re-layouts  27.5 us (9%)
  matrix products  23.6 us (8%)
  starting transfers between devices  19.1 us (6%)
  blocking collectives  15.8 us (5%)
    all_gather x1, waiting for transfers between devices, body(): row_block = lax.all_gather(slices, SEQ, axis=1, tiled=True)  69.3 us
    all_gather x1, waiting for transfers between devices, body(): gathered = lax.all_gather(normed, SEQ, axis=0, tiled=True)  51.6 us
    reduce_scatter x1, waiting for transfers between devices, body(): lax.psum_scatter(jnp.dot(row_block, out_weight, preferred_element_type=jn...  22.7 us
    ppermute x12, waiting for transfers between devices, prefix_over(): lax.ppermute(part, axis, [(i, (i + d) % peers) for i in range(peers)])  19.6 us
    all_to_all x1, blocking collectives, body(): lax.all_to_all(buffer.reshape(experts, capacity, columns), 'exp', split_a...  15.8 us
    ppermute x12, starting transfers between devices, prefix_over(): lax.ppermute(part, axis, [(i, (i + d) % peers) for i in range(peers)])  15.2 us
    dot_general x1, other arithmetic, body(): jnp.einsum('rd,rd->r', row_block, row_block, preferred_element_type=jnp.f...  7.08 us
    dot_general x1, matrix products, body(): lax.dot_general(w_gate, row_block, contract_last, preferred_element_type=...  6.96 us
  transfers between devices with their start and end apart: 18, of which 8 were waited for; matrix products, arithmetic and copies ran while one was open for 10% of the time, Pallas kernels for 0%

commit v1 on v0

--- a/solution.py
+++ b/solution.py
@@ -153,7 +153,9 @@
     )
     sources, entries, gathered_columns = received.shape
     slices = received.reshape(sources * entries, gathered_columns)
-    row_block = lax.all_gather(slices, SEQ, axis=1, tiled=True)
+    row_block = jnp.concatenate(
+        lax.all_to_all(jnp.stack([slices] * lax.axis_size(SEQ)), SEQ, 0, 0), axis=1
+    )
     squares = jnp.einsum("rd,rd->r", row_block, row_block, preferred_element_type=jnp.float32)
     gate_sum = lax.dot_general(w_gate, row_block, contract_last, preferred_element_type=jnp.float32)
     up_sum = lax.dot_general(w_up, row_block, contract_last, preferred_element_type=jnp.float32)

time: 313 us -> 402 us (1.28)
  blocking collectives: 15.8 us -> 168 us
  waiting for transfers between devices: 163 us -> 93.9 us
  local copies, waits for them, and re-layouts: 27.5 us -> 33 us
    all_to_all x0 -> x1, blocking collectives: none -> 153 us  [body(): lax.all_to_all(jnp.stack([slices] * lax.axis_size(SEQ)), SEQ, 0, 0)]
    all_gather x1 -> x0, waiting for transfers between devices: 69.3 us -> none  [body(): row_block = lax.all_gather(slices, SEQ, axis=1, tiled=True)]
    another operation x1 -> x3, local copies, waits for them, and re-layouts: 0.69 us -> 6.92 us  [the longest x2 6.24 us: body(): jnp.stack([slices] * lax.axis_size(SEQ))]
  transfers between devices with their start and end apart: 18 -> 17, of which waited for: 8 -> 7; matrix products, arithmetic and copies ran while one was open for 10% -> 8% of each run, Pallas kernels for 0% -> 0%
where the time goes in v1:
time: 402 us; the launch traced here: 400 us
  blocking collectives  168 us (42%)
  waiting for transfers between devices  93.9 us (23%)
  between operations  34 us (8%)
  local copies, waits for them, and re-layouts  33 us (8%)
  other arithmetic  28.5 us (7%)
  matrix products  23.6 us (6%)
  starting transfers between devices  19.1 us (5%)
    all_to_all x1, blocking collectives, body(): lax.all_to_all(jnp.stack([slices] * lax.axis_size(SEQ)), SEQ, 0, 0)  153 us
    all_gather x1, waiting for transfers between devices, body(): gathered = lax.all_gather(normed, SEQ, axis=0, tiled=True)  51.6 us
    reduce_scatter x1, waiting for transfers between devices, body(): lax.psum_scatter(jnp.dot(row_block, out_weight, preferred_element_type=jn...  22.7 us
    ppermute x12, waiting for transfers between devices, prefix_over(): lax.ppermute(part, axis, [(i, (i + d) % peers) for i in range(peers)])  19.6 us
    all_to_all x1, blocking collectives, body(): lax.all_to_all(buffer.reshape(experts, capacity, columns), 'exp', split_a...  15.8 us
    ppermute x12, starting transfers between devices, prefix_over(): lax.ppermute(part, axis, [(i, (i + d) % peers) for i in range(peers)])  15.2 us
  transfers between devices with their start and end apart: 17, of which 7 were waited for; matrix products, arithmetic and copies ran while one was open for 8% of the time, Pallas kernels for 0%

profile of v1, /device:TPU:1, one launch (start us, length us, event | category | flops | bytes accessed | tf_op | source)
XLA Modules:
  0.0 400.5 jit_solution(4496793939262456295)
XLA Ops:
  10.9 3.2 collective-permute-start
  17.0 2.4 fusion.36
  49.0 2.3 collective-permute-start.3
  55.4 2.5 collective-permute-start.6
  58.5 1.9 collective-permute-done.10
  62.0 7.3 %collective-permute-done.8 = f32[4,128,128]{2,1,0:T(8,128)S(1)} collective-permute-done((f32[4,128,128]{2,1,0:T(8,128)S(1)}, f32[4,128,128]{2,1,0:T(8,128)S(1)}, u32[]{:S(2)}, u32[]{:S(2)}) %collective-permute-start.8) | collective-permute-done | bytes 262176 | tf_op jit(solution)/shard_map/ppermute | solution.py:47
  69.6 2.8 collective-permute-start.12
  72.8 2.4 collective-permute-start.13
  75.2 3.5 collective-permute-done.12
  78.6 6.4 %collective-permute-done.11 = f32[4,128,128]{2,1,0:T(8,128)S(1)} collective-permute-done((f32[4,128,128]{2,1,0:T(8,128)S(1)}, f32[4,128,128]{2,1,0:T(8,128)S(1)}, u32[]{:S(2)}, u32[]{:S(2)}) %collective-permute-start.11) | collective-permute-done | bytes 262176 | tf_op jit(solution)/shard_map/ppermute | solution.py:47
  90.1 2.2 multiply_reduce_fusion
  93.2 51.6 %all-gather.2.cloned.1.call-done = bf16[2048,1024]{1,0:T(8,128)(2,1)} async-done(((bf16[64,1024]{1,0:T(8,128)(2,1)}), bf16[2048,1024]{1,0:T(8,128)(2,1)}) %all-gather.2.cloned.1.call-update) | async-done | bytes 4194320 | tf_op jit(solution)/shard_map/all_gather | solution.py:127
  144.8 5.0 %fusion.62 = f32[2048,192]{0,1:T(8,128)} fusion(bf16[2048,1024]{1,0:T(8,128)(2,1)} %all-gather.2.cloned.1.call-done, bf16[1024,192]{0,1:T(8,128)(2,1)} %param.13), kind=kOutput, calls=%fused_computation.128 | convolution fusion | flops 805306368 | bytes 6160384 | tf_op jit(solution)/shard_map/dot_general | solution.py:130
  156.3 2.2 reduce-window.6
  162.7 22.7 %reduce-scatter.2.cloned.1.call-done = f32[256,192]{0,1:T(8,128)} async-done(((f32[2048,192]{0,1:T(8,128)}), f32[256,192]{0,1:T(8,128)}) %reduce-scatter.2.cloned.1.call-update) | async-done | bytes 196624 | tf_op jit(solution)/shard_map/reduce_scatter | solution.py:129
  190.5 1.9 reshape.151
  192.3 3.5 scatter_custom_fusion
  195.9 2.0 copy.85
  197.9 15.8 %all_to_all.10 = bf16[8,128,192]{1,2,0:T(8,128)(2,1)S(1)} all-to-all(bf16[8,128,192]{1,2,0:T(8,128)(2,1)} %copy.85), channel_id=1, replica_groups=mesh['seq_0'=4,'seq_1'=4,'seq_2'=2,'exp'=8] {'exp'}, dimensions={0} | all-to-all | bytes 786432 | tf_op jit(solution)/shard_map/all_to_all | solution.py:151
  213.7 6.2 %stack.203 = bf16[32,1024,192]{1,2,0:T(8,128)(2,1)} broadcast(bf16[1024,192]{0,1:T(8,128)(2,1)S(1)} %copy_bitcast_fusion), dimensions={1,2} | broadcast | bytes 12976128 | tf_op jit(solution)/shard_map/stack | solution.py:157
  219.9 152.6 %all_to_all.11 = bf16[32,1024,192]{1,2,0:T(8,128)(2,1)} all-to-all(bf16[32,1024,192]{1,2,0:T(8,128)(2,1)} %stack.203), channel_id=1, replica_groups=mesh['seq_0'=4,'seq_1'=4,'seq_2'=2,'exp'=8] {'seq_0','seq_1','seq_2'}, dimensions={0} | all-to-all | bytes 25165824 | tf_op jit(solution)/shard_map/all_to_all | solution.py:157
  372.4 7.1 %fusion = f32[1024]{0:T(1024)S(1)} fusion(bf16[32,1024,192]{1,2,0:T(8,128)(2,1)} %all_to_all.11), kind=kLoop, calls=%fused_computation.2 | loop fusion | flops 18873344 | bytes 12587008 | tf_op jit(solution)/shard_map/rd,rd->r/dot_general | solution.py:159
  379.6 7.0 %fusion.17 = f32[288,1024]{1,0:T(8,128)S(1)} fusion(bf16[1024,6144]{0,1:T(8,128)(2,1)} %bitcast.152, bf16[1,288,6144]{2,1,0:T(8,128)(2,1)S(1)} %copy-done, f32[1024]{0:T(1024)S(1)} %add_rsqrt_fusion), kind=kOutput, calls=%fused_computation.11 | convolution fusion | flops 3624173568 | bytes 17305600 | tf_op jit(solution)/shard_map/dot_general | solution.py:160
  388.7 4.9 %fusion.23 = bf16[1,288,1024]{2,1,0:T(8,128)(2,1)} fusion(bf16[1024,6144]{0,1:T(8,128)(2,1)S(1)} %bitcast.153, bf16[1,288,6144]{2,1,0:T(8,128)(2,1)S(1)} %copy-done.5, f32[288,1024]{1,0:T(8,128)S(1)} %fusion.17, f32[1024]{0:T(1024)S(1)} %add_rsqrt_fusion), kind=kOutput, calls=%fused_computation.13 | convolution fusion | flops 3625943040 | bytes 17895424 | tf_op jit(solution)/shard_map/dot_general | solution.py:161
  (97 shorter events, 47.1 us)
Async XLA Ops:
  7.2 372.4 %copy-start = (bf16[1,288,6144]{2,1,0:T(8,128)(2,1)S(1)}, bf16[1,288,6144]{2,1,0:T(8,128)(2,1)}, u32[]{:S(2)}) copy-start(bf16[1,288,6144]{2,1,0:T(8,128)(2,1)} %param.16) | copy-start | bytes 10616836
  7.2 137.6 %all-gather.2.cloned.1.call-start = ((), (), s32[]{:S(2)}) async-start(), calls=%async_computation.3 | async-start | bytes 4325376 | tf_op jit(solution)/shard_map/all_gather | solution.py:127
  10.9 35.7 %collective-permute-start = (f32[8]{0:T(128)S(1)}, f32[8]{0:T(128)S(1)}, u32[]{:S(2)}, u32[]{:S(2)}) collective-permute-start(f32[8]{0:T(128)S(1)} %fusion.59), channel_id=1, source_target_pairs={{0,8},{8,0},{1,9},{9,1},{2,10},{10,2},{3,11},{11,3},{4,12},{12,4},... | collective-permute-start | bytes 104 | tf_op jit(solution)/shard_map/ppermute | solution.py:40
  19.5 31.9 %collective-permute-start.7 = (f32[8,128,128]{2,1,0:T(8,128)}, f32[8,128,128]{2,1,0:T(8,128)}, u32[]{:S(2)}, u32[]{:S(2)}) collective-permute-start(f32[8,128,128]{2,1,0:T(8,128)} %fusion.36), channel_id=1, source_target_pairs={{0,8},{8,0},{1,9},{9,1},{2,10},{10,2},{3,11},{11,3},{4,12},{12,4},... | collective-permute-start | bytes 1572872 | tf_op jit(solution)/shard_map/ppermute | solution.py:40
  46.6 40.5 %copy-start.3 = (bf16[64,1024]{1,0:T(8,128)(2,1)S(1)}, bf16[64,1024]{1,0:T(8,128)(2,1)}, u32[]{:S(2)}) copy-start(bf16[64,1024]{1,0:T(8,128)(2,1)} %param.10) | copy-start | bytes 393220
  46.6 40.5 %copy-start.6 = (bf16[64,1024]{1,0:T(8,128)(2,1)S(1)}, bf16[64,1024]{1,0:T(8,128)(2,1)}, u32[]{:S(2)}) copy-start(bf16[64,1024]{1,0:T(8,128)(2,1)} %param.9) | copy-start | bytes 393220
  47.4 7.4 %collective-permute-start.2 = (f32[4]{0:T(128)S(1)}, f32[4]{0:T(128)S(1)}, u32[]{:S(2)}, u32[]{:S(2)}) collective-permute-start(f32[4]{0:T(128)S(1)} %dynamic_slice.6), channel_id=1, source_target_pairs={{0,32},{16,48},{32,0},{48,16},{1,33},{17,49},{33,1},{49,17},{2,34}... | collective-permute-start | bytes 56 | tf_op jit(solution)/shard_map/ppermute | solution.py:47
  48.6 6.7 %collective-permute-start.1 = (f32[4]{0:T(128)S(1)}, f32[4]{0:T(128)S(1)}, u32[]{:S(2)}, u32[]{:S(2)}) collective-permute-start(f32[4]{0:T(128)S(1)} %dynamic_slice.6), channel_id=1, source_target_pairs={{0,16},{16,32},{32,48},{48,0},{1,17},{17,33},{33,49},{49,1},{2,18}... | collective-permute-start | bytes 56 | tf_op jit(solution)/shard_map/ppermute | solution.py:47
  49.0 6.3 %collective-permute-start.3 = (f32[4]{0:T(128)S(1)}, f32[4]{0:T(128)S(1)}, u32[]{:S(2)}, u32[]{:S(2)}) collective-permute-start(f32[4]{0:T(128)S(1)} %dynamic_slice.6), channel_id=1, source_target_pairs={{0,48},{16,0},{32,16},{48,32},{1,49},{17,1},{33,17},{49,33},{2,50}... | collective-permute-start | bytes 56 | tf_op jit(solution)/shard_map/ppermute | solution.py:47
  52.5 16.9 %copy-start.2 = (f32[8,128,128]{2,1,0:T(8,128)}, f32[8,128,128]{2,1,0:T(8,128)S(1)}, u32[]{:S(2)}) copy-start(f32[8,128,128]{2,1,0:T(8,128)S(1)} %broadcast_select_fusion) | copy-start | bytes 1572868
  53.8 6.5 %collective-permute-start.10 = (f32[4,128,128]{2,1,0:T(8,128)S(1)}, f32[4,128,128]{2,1,0:T(8,128)S(1)}, u32[]{:S(2)}, u32[]{:S(2)}) collective-permute-start(f32[4,128,128]{2,1,0:T(8,128)S(1)} %fusion.30), channel_id=1, source_target_pairs={{0,48},{16,0},{32,16},{48,32},{1,49},{17,1},{33,17},{49,33},{2,50}... | collective-permute-start | bytes 786440 | tf_op jit(solution)/shard_map/ppermute | solution.py:47
  53.9 8.1 %collective-permute-start.9 = (f32[4,128,128]{2,1,0:T(8,128)S(1)}, f32[4,128,128]{2,1,0:T(8,128)S(1)}, u32[]{:S(2)}, u32[]{:S(2)}) collective-permute-start(f32[4,128,128]{2,1,0:T(8,128)S(1)} %fusion.30), channel_id=1, source_target_pairs={{0,32},{16,48},{32,0},{48,16},{1,33},{17,49},{33,1},{49,17},{2,34}... | collective-permute-start | bytes 786440 | tf_op jit(solution)/shard_map/ppermute | solution.py:47
  54.9 14.5 %collective-permute-start.8 = (f32[4,128,128]{2,1,0:T(8,128)S(1)}, f32[4,128,128]{2,1,0:T(8,128)S(1)}, u32[]{:S(2)}, u32[]{:S(2)}) collective-permute-start(f32[4,128,128]{2,1,0:T(8,128)S(1)} %fusion.30), channel_id=1, source_target_pairs={{0,16},{16,32},{32,48},{48,0},{1,17},{17,33},{33,49},{49,1},{2,18}... | collective-permute-start | bytes 786440 | tf_op jit(solution)/shard_map/ppermute | solution.py:47
  55.4 17.3 %collective-permute-start.6 = (f32[4]{0:T(128)S(1)}, f32[4]{0:T(128)S(1)}, u32[]{:S(2)}, u32[]{:S(2)}) collective-permute-start(f32[4]{0:T(128)S(1)} %get-tuple-element.19), channel_id=1, source_target_pairs={{0,192},{64,0},{128,64},{192,128},{1,193},{65,1},{129,65},{193,129... | collective-permute-start | bytes 56 | tf_op jit(solution)/shard_map/ppermute | solution.py:47
  57.9 17.2 %collective-permute-start.5 = (f32[4]{0:T(128)S(1)}, f32[4]{0:T(128)S(1)}, u32[]{:S(2)}, u32[]{:S(2)}) collective-permute-start(f32[4]{0:T(128)S(1)} %get-tuple-element.19), channel_id=1, source_target_pairs={{0,128},{64,192},{128,0},{192,64},{1,129},{65,193},{129,1},{193,65... | collective-permute-start | bytes 56 | tf_op jit(solution)/shard_map/ppermute | solution.py:47
  60.3 14.8 %collective-permute-start.4 = (f32[4]{0:T(128)S(1)}, f32[4]{0:T(128)S(1)}, u32[]{:S(2)}, u32[]{:S(2)}) collective-permute-start(f32[4]{0:T(128)S(1)} %get-tuple-element.19), channel_id=1, source_target_pairs={{0,64},{64,128},{128,192},{192,0},{1,65},{65,129},{129,193},{193,1... | collective-permute-start | bytes 56 | tf_op jit(solution)/shard_map/ppermute | solution.py:47
  69.6 9.0 %collective-permute-start.12 = (f32[4,128,128]{2,1,0:T(8,128)S(1)}, f32[4,128,128]{2,1,0:T(8,128)S(1)}, u32[]{:S(2)}, u32[]{:S(2)}) collective-permute-start(f32[4,128,128]{2,1,0:T(8,128)S(1)} %select_add_fusion.1), channel_id=1, source_target_pairs={{0,128},{64,192},{128,0},{192,64},{1,129},{65,193},{129,1},{193,65... | collective-permute-start | bytes 786440 | tf_op jit(solution)/shard_map/ppermute | solution.py:47
  72.4 12.6 %collective-permute-start.11 = (f32[4,128,128]{2,1,0:T(8,128)S(1)}, f32[4,128,128]{2,1,0:T(8,128)S(1)}, u32[]{:S(2)}, u32[]{:S(2)}) collective-permute-start(f32[4,128,128]{2,1,0:T(8,128)S(1)} %select_add_fusion.1), channel_id=1, source_target_pairs={{0,64},{64,128},{128,192},{192,0},{1,65},{65,129},{129,193},{193,1... | collective-permute-start | bytes 786440 | tf_op jit(solution)/shard_map/ppermute | solution.py:47
  72.8 12.3 %collective-permute-start.13 = (f32[4,128,128]{2,1,0:T(8,128)S(1)}, f32[4,128,128]{2,1,0:T(8,128)S(1)}, u32[]{:S(2)}, u32[]{:S(2)}) collective-permute-start(f32[4,128,128]{2,1,0:T(8,128)S(1)} %select_add_fusion.1), channel_id=1, source_target_pairs={{0,192},{64,0},{128,64},{192,128},{1,193},{65,1},{129,65},{193,129... | collective-permute-start | bytes 786440 | tf_op jit(solution)/shard_map/ppermute | solution.py:47
  86.5 3.6 collective-permute-start.14
  93.1 56.7 %copy-start.4 = (s32[256,2]{0,1:T(2,128)S(1)}, s32[256,2]{0,1:T(2,128)}, u32[]{:S(2)}) copy-start(s32[256,2]{0,1:T(2,128)} %param.15) | copy-start | bytes 6148
  93.1 92.3 %reduce-scatter.2.cloned.1.call-start = ((), (), s32[]{:S(2)}) async-start(), calls=%async_computation.4 | async-start | bytes 1769472 | tf_op jit(solution)/shard_map/reduce_scatter | solution.py:129
  379.5 8.2 %copy-start.1 = (bf16[32,1024,192]{1,2,0:T(8,128)(2,1)S(1)}, bf16[32,1024,192]{1,2,0:T(8,128)(2,1)}, u32[]{:S(2)}) copy-start(bf16[32,1024,192]{1,2,0:T(8,128)(2,1)} %all_to_all.11) | copy-start | bytes 37748740
  379.6 9.2 %copy-start.5 = (bf16[1,288,6144]{2,1,0:T(8,128)(2,1)S(1)}, bf16[1,288,6144]{2,1,0:T(8,128)(2,1)}, u32[]{:S(2)}) copy-start(bf16[1,288,6144]{2,1,0:T(8,128)(2,1)} %param.17) | copy-start | bytes 10616836
Sparse Core Ops, SparseCore 0:
  93.2 51.5 all-gather.1
  149.9 35.4 reduce-scatter.1
